TPU v7x, 32 devices: a whole 2x2x4 slice. The times are simulated.
32 devices in a mesh: groups: 2 (over x), seq: 16 (over z, y, core).
Axes of the slice: x: 2, y: 2, z: 4, core: 2. Of those that a mesh axis runs over, the one named last changes fastest.
Arguments:
- query: bfloat16 [4096, 1024], P(('groups', 'seq')), parts along dimension 0, as said below
- keys: bfloat16 [4096, 1024], P(('groups', 'seq')), parts along dimension 0, as said below
- values: bfloat16 [4096, 1024], P(('groups', 'seq')), parts along dimension 0, may hold values from -6 to 6
- out_weight: bfloat16 [1024, 2048], P('seq'), may hold values from -0.1875 to 0.1875
- grad_out: bfloat16 [4096, 2048], P(('groups', 'seq')), parts along dimension 0, may hold values from -6 to 6
- global_blocks: int32 [4], P('groups'), parts along dimension 0, may hold values from 0 to 15
- random_blocks: int32 [32, 3], P(('groups', 'seq')), parts along dimension 0, may hold values from 0 to 15, as said below
Outputs:
- layer_out: bfloat16 [4096, 2048], P(('groups', 'seq')), parts along dimension 0
- grad_query: bfloat16 [4096, 1024], P(('groups', 'seq')), parts along dimension 0
- grad_keys: bfloat16 [4096, 1024], P(('groups', 'seq')), parts along dimension 0
- grad_values: bfloat16 [4096, 1024], P(('groups', 'seq')), parts along dimension 0
- grad_weight: float32 [2048, 2048], P(('groups', 'seq')), parts along dimension 0
There are 2 independent parts, one for each index of `groups`. A program takes and returns all parts, laid end to end along the dimension named above; an argument that names none is the same for every part. Nothing has to cross between parts.
Inputs may be any that keep to these rules, and one draw needn't show every extreme that they name: `random_blocks`: random block r of query block b lies on the device that holds b or on a device beside it: it is at least max(b - 1, 0) * 1 and below min(b + 2, 16). `query`: entries lie between -12 and 12. `keys`: entries lie between -6 and 6.
All inputs are finite; a program needn't handle non-finite values.
Results may differ from a plain program's by a relative error of at most 0.012.
Values may be sent and summed in bfloat16 or wider, within the bound.
No kernel may reach another device: no remote copies, remote signals or barrier semaphores. Data moves between devices by JAX's collectives and lax.ppermute only.
A program may use at most 128 MiB of HBM per device.

v0:
```python
import math
import jax
import jax.numpy as jnp
from jax import lax
from jax.sharding import PartitionSpec as P

H = 8
BLK = 128
NEG_FILL = -1e30


def extended_2(shard, sides, width):
    for axis, dim in sides:
        count, length = (lax.axis_size(axis), shard.shape[dim])
        up = [(i, (i + 1) % count) for i in range(count - 1)]
        down = [(j, i) for i, j in up]
        last = lax.slice_in_dim(shard, length - width, length, axis=dim)
        initial = lax.slice_in_dim(shard, 0, width, axis=dim)
        before = lax.ppermute(last, axis, up)
        after = lax.ppermute(initial, axis, down)
        shard = jnp.concatenate([before, shard, after], axis=dim)
    return shard


def spread(shard, axis, root):
    mine = lax.axis_index(axis) == root
    return lax.psum(jnp.where(mine, shard, jnp.zeros_like(shard)), axis)


def window_and_random(random_rows, device, blocks_dev, total_blocks):
    local_ids = jnp.arange(blocks_dev, dtype=jnp.int32)
    global_ids = device * blocks_dev + local_ids
    offsets = jnp.array([-1, 0, 1], dtype=jnp.int32)
    neighbour_ids = global_ids[:, None] + offsets[None, :]
    window_index = local_ids[:, None] + blocks_dev + offsets[None, :]
    window_live = (neighbour_ids >= 0) & (neighbour_ids < total_blocks)
    random_index = random_rows - (device - 1) * blocks_dev
    ext_index = jnp.concatenate([window_index, random_index], axis=1)
    live_local = jnp.concatenate(
        [window_live, jnp.ones(random_rows.shape, dtype=jnp.bool_)], axis=1
    )
    return (ext_index, live_local)


def choose_blocks(extended, global_kv, ext_index, live_local, blocks_dev):
    feature_count = extended.shape[2]
    ext_blocks = extended.reshape(2, 3 * blocks_dev, BLK, feature_count)
    local_sel = jnp.take(ext_blocks, ext_index, axis=1)
    global_count = global_kv.shape[0]
    global_sel = jnp.swapaxes(global_kv, 0, 1)[:, None]
    chosen = jnp.concatenate([local_sel, global_sel], axis=2)
    listed = chosen.shape[2]
    chosen = chosen.reshape(2, blocks_dev, listed * BLK, H, feature_count // H)
    live = jnp.concatenate(
        [live_local, jnp.ones((blocks_dev, global_count), dtype=jnp.bool_)], axis=1
    )
    live_rows = jnp.repeat(live, BLK, axis=1)
    return (chosen[0], chosen[1], live_rows)


def attend_blocks(query_blocks, chosen_keys, chosen_values, live_rows):
    score_scale = 1.0 / math.sqrt(query_blocks.shape[-1])
    scores = (
        jnp.einsum("qihd,qjhd->qhij", query_blocks, chosen_keys, preferred_element_type=jnp.float32)
        * score_scale
    )
    scores = jnp.where(live_rows[:, None, None, :], scores, NEG_FILL)
    row_top = jnp.max(scores, axis=-1, keepdims=True)
    raised = jnp.exp(scores - row_top)
    soft_weights = raised / jnp.sum(raised, axis=-1, keepdims=True)
    rounded_weights = soft_weights.astype(jnp.bfloat16)
    mixed_out = jnp.einsum(
        "qhij,qjhd->qihd", rounded_weights, chosen_values, preferred_element_type=jnp.float32
    )
    return (soft_weights, rounded_weights, mixed_out.astype(jnp.bfloat16))


def attend_backward(
    query_blocks, chosen_keys, chosen_values, soft_weights, rounded_weights, upstream_blocks
):
    score_scale = 1.0 / math.sqrt(query_blocks.shape[-1])
    grad_chosen_values = jnp.einsum(
        "qhij,qihd->qjhd", rounded_weights, upstream_blocks, preferred_element_type=jnp.float32
    )
    grad_weights = jnp.einsum(
        "qihd,qjhd->qhij", upstream_blocks, chosen_values, preferred_element_type=jnp.float32
    )
    row_delta = jnp.sum(soft_weights * grad_weights, axis=-1, keepdims=True)
    grad_scores = (score_scale * soft_weights * (grad_weights - row_delta)).astype(jnp.bfloat16)
    grad_query_blocks = jnp.einsum(
        "qhij,qjhd->qihd", grad_scores, chosen_keys, preferred_element_type=jnp.float32
    )
    grad_chosen_keys = jnp.einsum(
        "qhij,qihd->qjhd", grad_scores, query_blocks, preferred_element_type=jnp.float32
    )
    return (grad_query_blocks, grad_chosen_keys, grad_chosen_values)


def fold_gradients(grad_chosen_keys, grad_chosen_values, ext_index, blocks_dev):
    stacked = jnp.stack([grad_chosen_keys, grad_chosen_values])
    listed_local = ext_index.shape[1]
    feature_count = stacked.shape[3] * stacked.shape[4]
    stacked = stacked.reshape(2, blocks_dev, -1, BLK * feature_count)
    local_part = stacked[:, :, :listed_local].reshape(
        2, blocks_dev * listed_local, BLK * feature_count
    )
    one_hot = (
        ext_index.reshape(-1)[:, None] == jnp.arange(3 * blocks_dev, dtype=jnp.int32)[None, :]
    ).astype(jnp.float32)
    grad_ext = jnp.einsum("sj,ksx->kjx", one_hot, local_part, precision=lax.Precision.HIGHEST)
    grad_ext = grad_ext.reshape(2, 3 * blocks_dev * BLK, feature_count)
    grad_global = jnp.sum(stacked[:, :, listed_local:], axis=1).reshape(2, -1, BLK, feature_count)
    return (grad_ext, grad_global)


def local(query, keys, values, out_weight, grad_out, global_blocks, random_blocks):
    tok_rows = query.shape[0]
    feature_count = query.shape[1]
    blocks_dev = tok_rows // BLK
    device = lax.axis_index("seq")
    total_blocks = blocks_dev * lax.axis_size("seq")
    paired = jnp.stack([keys, values])
    extended = extended_2(paired, (("seq", 1),), tok_rows)
    fetched = []
    for global_slot in range(global_blocks.shape[0]):
        block_id = global_blocks[global_slot]
        owner_index = block_id // blocks_dev
        fetched.append(spread(paired, "seq", owner_index))
    global_kv = jnp.stack(fetched)
    ext_index, live_local = window_and_random(random_blocks, device, blocks_dev, total_blocks)
    chosen_keys, chosen_values, live_rows = choose_blocks(
        extended, global_kv, ext_index, live_local, blocks_dev
    )
    query_blocks = query.reshape(blocks_dev, BLK, H, feature_count // H)
    soft_weights, rounded_weights, mixed_out = attend_blocks(
        query_blocks, chosen_keys, chosen_values, live_rows
    )
    attn_out = mixed_out.reshape(tok_rows, feature_count)
    columns = attn_out
    layer_sum = jnp.dot(
        columns,
        lax.all_gather(out_weight, "seq", axis=0, tiled=True),
        preferred_element_type=jnp.float32,
    )
    upstream_sum = lax.dot_general(
        grad_out,
        lax.all_gather(out_weight, "seq", axis=0, tiled=True),
        (((1,), (1,)), ((), ())),
        preferred_element_type=jnp.float32,
    )
    layer_out = layer_sum.astype(jnp.bfloat16)
    upstream_blocks = upstream_sum.astype(jnp.bfloat16).reshape(
        blocks_dev, BLK, H, feature_count // H
    )
    columns = attn_out
    grad_weight = lax.psum_scatter(
        lax.dot_general(
            columns, grad_out, (((0,), (0,)), ((), ())), preferred_element_type=jnp.float32
        ),
        "seq",
        scatter_dimension=0,
        tiled=True,
    )
    grad_query_blocks, grad_chosen_keys, grad_chosen_values = attend_backward(
        query_blocks, chosen_keys, chosen_values, soft_weights, rounded_weights, upstream_blocks
    )
    grad_ext, grad_global = fold_gradients(
        grad_chosen_keys, grad_chosen_values, ext_index, blocks_dev
    )
    rim_grads = jnp.concatenate(
        [grad_ext[:, :tok_rows], grad_ext[:, 2 * tok_rows :]], axis=1
    ).astype(jnp.bfloat16)
    arrived = extended_2(rim_grads, (("seq", 1),), tok_rows)
    global_total = lax.psum(grad_global, "seq")
    owned_mask = (
        global_blocks[:, None]
        == device * blocks_dev + jnp.arange(blocks_dev, dtype=jnp.int32)[None, :]
    ).astype(jnp.float32)
    owned_sum = jnp.einsum(
        "gj,kgx->kjx",
        owned_mask,
        global_total.reshape(2, owned_mask.shape[0], -1),
        precision=lax.Precision.HIGHEST,
    )
    grad_paired = grad_ext[:, tok_rows : 2 * tok_rows] + arrived[:, :tok_rows].astype(jnp.float32)
    grad_paired = grad_paired + arrived[:, 3 * tok_rows :].astype(jnp.float32)
    grad_paired = grad_paired + owned_sum.reshape(2, tok_rows, feature_count)
    grad_paired = grad_paired.astype(jnp.bfloat16)
    grad_query = grad_query_blocks.reshape(tok_rows, feature_count).astype(jnp.bfloat16)
    return (layer_out, grad_query, grad_paired[0], grad_paired[1], grad_weight)


def solution(mesh):
    placed = (
        P(("groups", "seq"), None),
        P(("groups", "seq"), None),
        P(("groups", "seq"), None),
        P("seq", None),
        P(("groups", "seq"), None),
        P("groups"),
        P(("groups", "seq"), None),
    )
    return jax.shard_map(
        local,
        mesh=mesh,
        in_specs=placed,
        out_specs=(
            P(("groups", "seq"), None),
            P(("groups", "seq"), None),
            P(("groups", "seq"), None),
            P(("groups", "seq"), None),
            P(("groups", "seq"), None),
        ),
        check_vma=False,
    )
```

profile of v0, /device:TPU:0, one launch (start us, length us, event | category | flops | bytes accessed | tf_op | source)
XLA Modules:
  0.0 429.1 jit_solution(10546698557166395422)
XLA Ops:
  7.2 0.0 copy-start
  7.2 0.0 copy-start.12
  7.2 0.0 copy-start.11
  7.2 0.0 all-reduce.6.cloned.1.call-start
  7.3 1.4 fusion.36
  10.0 2.1 select_bitcast_fusion.1
  12.1 0.0 all-reduce.6.cloned.1.call-update
  12.1 0.0 all-gather.2.cloned.1.call-start
  12.1 0.7 all-gather.2.cloned.1.call-update
  12.8 0.0 all-reduce.4.cloned.1.call-start
  12.9 1.3 collective-permute-start.1
  14.2 3.8 collective-permute-start
  18.0 0.1 fusion.30
  18.1 0.1 compare_and_fusion
  18.2 0.1 fusion.28
  18.3 0.1 broadcast_bitcast_fusion
  18.4 0.5 collective-permute-done
  18.9 1.2 pad_maximum_fusion.2
  20.0 2.5 gather_fusion
  22.5 89.4 %all-reduce.6.cloned.1.call-done = (bf16[1,2,128,1024]{3,2,1,0:T(8,128)(2,1)}, bf16[1,2,128,1024]{3,2,1,0:T(8,128)(2,1)}) async-done(((bf16[1,2,128,1024]{3,2,1,0:T(8,128)(2,1)}, bf16[1,2,128,1024]{3,2,1,0:T(8,128)(2,1)}), (bf16[1,2,128,1024]{3,2,1,0:T(8,128)(2,1)}, bf16[1,2,128,1024]{3,2,1,0:T(8,128)(2,1)})) %all-reduce.6.cloned.1.call-update) | async-done | bytes 1048592 | tf_op jit(solution)/shard_map/psum | solution.py:27
  111.9 1.3 maximum_bitcast_fusion.2
  113.2 2.3 bitcast_select_fusion
  115.5 1.6 pad_maximum_fusion.1
  117.1 0.6 copy.57
  117.7 3.0 copy.52
  120.7 3.6 copy.58
  124.3 3.3 copy.34
  127.6 0.8 fusion.22
  128.4 3.4 fusion.37
  131.8 32.2 %all-gather.2.cloned.1.call-done = bf16[1024,2048]{1,0:T(8,128)(2,1)} async-done(((bf16[64,2048]{1,0:T(8,128)(2,1)}), bf16[1024,2048]{1,0:T(8,128)(2,1)}) %all-gather.2.cloned.1.call-update) | async-done | bytes 4194320 | tf_op jit(solution)/shard_map/all_gather | solution.py:142
  164.0 3.7 convolution_convert_fusion.3
  167.7 0.2 copy.55
  167.9 5.0 %convolution_bitcast_fusion.1 = f32[1,1024,8,128]{1,3,2,0:T(8,128)} fusion(bf16[128,8,128]{0,2,1:T(8,128)(2,1)S(1)} %bitcast.154, f32[8,128,1024]{1,2,0:T(8,128)} %get-tuple-element.29, f32[8,128]{1,0:T(8,128)S(1)} %get-tuple-element.28), kind=kOutput, calls=%fused_computation.19 | convolution fusion | flops 270532608 | bytes 8654848 | tf_op jit(solution)/shard_map/qhij,qihd->qjhd/dot_general | solution.py:82
  172.9 3.1 multiply_reduce_fusion
  176.0 5.4 %copy.40 = f32[1,1024,8,128]{3,2,1,0:T(8,128)} copy(f32[1,1024,8,128]{1,3,2,0:T(8,128)} %convolution_bitcast_fusion.1) | data formatting | bytes 8388608 | tf_op jit(solution)/shard_map/qhij,qihd->qjhd/transpose | solution.py:82
  181.3 4.9 %stack.34 = f32[1,1,8,131072]{3,2,1,0:T(8,128)} reshape(f32[1,1024,8,128]{3,2,1,0:T(8,128)} %copy.40) | data formatting | bytes 8388608 | tf_op jit(solution)/shard_map/stack | solution.py:100
  186.2 4.2 multiply_convert_fusion
  190.4 0.7 convolution_bitcast_fusion.2
  191.1 0.6 copy-done.1
  191.7 4.4 %copy.37 = f32[1,1024,8,128]{3,2,1,0:T(8,128)} copy(f32[1,1024,8,128]{3,1,2,0:T(8,128)S(1)} %convolution_bitcast_fusion.2) | data formatting | bytes 8388608 | tf_op jit(solution)/shard_map/qhij,qihd->qjhd/transpose | solution.py:93
  196.1 4.9 %stack.33 = f32[1,1,8,131072]{3,2,1,0:T(8,128)} reshape(f32[1,1024,8,128]{3,2,1,0:T(8,128)} %copy.37) | data formatting | bytes 8388608 | tf_op jit(solution)/shard_map/stack | solution.py:100
  201.0 5.7 %fusion.10 = f32[2,131072,2]{1,2,0:T(2,128)} fusion(f32[1,1,8,131072]{3,2,0,1:T(8,128)} %bitcast.138, f32[1,1,8,131072]{3,2,0,1:T(8,128)} %bitcast.140), kind=kLoop, calls=%fused_computation.23 | loop fusion | flops 524288 | bytes 10485760 | tf_op jit(solution)/shard_map/gj,kgx->kjx/dot_general | solution.py:179
  206.7 4.0 dot_general.56
  210.8 0.0 all-reduce.4.cloned.1.call-update
  210.8 0.3 reduce-scatter.2.cloned.1.call-start
  211.0 3.6 convolution_convert_fusion.2
  214.6 4.5 %fusion.38 = f32[1024,2048]{1,0:T(8,128)} fusion(bf16[128,1024]{0,1:T(8,128)(2,1)S(1)} %bitcast.147, bf16[128,2048]{1,0:T(8,128)(2,1)S(1)} %copy-done), kind=kOutput, calls=%fused_computation.75 | convolution fusion | flops 536870912 | bytes 9175040 | tf_op jit(solution)/shard_map/dot_general | solution.py:157
  219.1 0.0 reduce-scatter.2.cloned.1.call-update
  219.1 0.6 copy-done.10
  219.7 0.1 add_bitcast_fusion
  219.8 2.3 convolution_convert_fusion.1
  222.1 0.9 copy.43
  223.0 9.7 %convolution_bitcast_fusion = f32[2,3,131072]{2,1,0:T(4,128)} fusion(f32[1,1,8,131072]{3,2,0,1:T(8,128)} %bitcast.139, f32[1,1,8,131072]{3,2,0,1:T(8,128)} %bitcast.141, s32[6]{0:T(128)S(1)} %add_bitcast_fusion), kind=kOutput, calls=%fused_computation.2 | convolution fusion | flops 58195984 | bytes 11534360 | tf_op jit(solution)/shard_map/sj,ksx->kjx/dot_general | solution.py:110
  232.7 5.1 %reshape.362 = f32[2,384,1024]{2,1,0:T(8,128)} reshape(f32[2,3,131072]{2,1,0:T(4,128)} %convolution_bitcast_fusion) | data formatting | bytes 6291456 | tf_op jit(solution)/shard_map/reshape | solution.py:111
  237.8 2.3 convert.6
  240.1 0.1 fusion.35
  240.2 1.3 collective-permute-start.3
  241.5 3.3 collective-permute-start.2
  244.9 1.5 convolution_convert_fusion
  246.4 67.3 %all-reduce.4.cloned.1.call-done = f32[2,128,1024,2]{2,1,3,0:T(8,128)} async-done(((f32[2,128,1024,2]{2,1,3,0:T(8,128)}), f32[2,128,1024,2]{2,1,3,0:T(8,128)}) %all-reduce.4.cloned.1.call-update) | async-done | bytes 2097168 | tf_op jit(solution)/shard_map/psum | solution.py:174
  313.7 6.6 %fusion.13 = f32[1,2,128,1024]{3,0,2,1:T(1,128)S(1)} fusion(f32[2,128,1024,2]{2,1,3,0:T(8,128)} %all-reduce.4.cloned.1.call-done, s32[2]{0:T(128)S(1)} %copy-done.8, s32[]{:T(128)S(6)} %axis_index.8), kind=kOutput, calls=%fused_computation.28 | convolution fusion | flops 6291458 | bytes 3145740 | tf_op jit(solution)/shard_map/gj,kgx->kjx/dot_general | solution.py:179
  320.3 1.7 fusion.18
  322.0 0.8 slice_bitcast_fusion
  322.8 99.8 %reduce-scatter.2.cloned.1.call-done = f32[64,2048]{1,0:T(8,128)} async-done(((f32[1024,2048]{1,0:T(8,128)}), f32[64,2048]{1,0:T(8,128)}) %reduce-scatter.2.cloned.1.call-update) | async-done | bytes 524304 | tf_op jit(solution)/shard_map/reduce_scatter | solution.py:156
  (32 shorter events, 0.1 us)
Async XLA Ops:
  7.2 156.8 %copy-start = (bf16[128,2048]{1,0:T(8,128)(2,1)S(1)}, bf16[128,2048]{1,0:T(8,128)(2,1)}, u32[]{:S(2)}) copy-start(bf16[128,2048]{1,0:T(8,128)(2,1)} %param.12) | copy-start | bytes 1572868
  7.2 10.8 %copy-start.12 = (s32[1,3,1]{1,2,0:T(1,128)S(1)}, s32[1,3,1]{1,2,0:T(1,128)}, u32[]{:S(2)}) copy-start(s32[1,3,1]{1,2,0:T(1,128)} %constant.63) | copy-start | bytes 40
  7.2 10.9 %copy-start.11 = (s32[3]{0:T(128)S(1)}, s32[3]{0:T(128)}, u32[]{:S(2)}) copy-start(s32[3]{0:T(128)} %constant.60.clone) | copy-start | bytes 40
  7.2 11.7 %copy-start.6 = (bf16[128,1024]{1,0:T(8,128)(2,1)S(1)}, bf16[128,1024]{1,0:T(8,128)(2,1)}, u32[]{:S(2)}) copy-start(bf16[128,1024]{1,0:T(8,128)(2,1)} %param.10) | copy-start | bytes 786436
  7.2 11.7 %copy-start.7 = (bf16[128,1024]{1,0:T(8,128)(2,1)S(1)}, bf16[128,1024]{1,0:T(8,128)(2,1)}, u32[]{:S(2)}) copy-start(bf16[128,1024]{1,0:T(8,128)(2,1)} %param.9) | copy-start | bytes 786436
  7.2 10.8 %copy-start.9 = (s32[1,3]{1,0:T(1,128)S(1)}, s32[1,3]{1,0:T(1,128)}, u32[]{:S(2)}) copy-start(s32[1,3]{1,0:T(1,128)} %param.14) | copy-start | bytes 40
  7.2 104.7 %all-reduce.6.cloned.1.call-start = ((), (), s32[]{:S(2)}) async-start(), calls=%async_computation.4 | async-start | bytes 2097152 | tf_op jit(solution)/shard_map/psum | solution.py:27
  12.1 151.9 %all-gather.2.cloned.1.call-start = ((), (), s32[]{:S(2)}) async-start(), calls=%async_computation.1 | async-start | bytes 4456448 | tf_op jit(solution)/shard_map/all_gather | solution.py:142
  12.8 300.8 %all-reduce.4.cloned.1.call-start = ((), (), s32[]{:S(2)}) async-start(), calls=%async_computation.2 | async-start | bytes 4194304 | tf_op jit(solution)/shard_map/psum | solution.py:174
  12.9 5.5 %collective-permute-start.1 = (bf16[2,128,1024]{2,1,0:T(8,128)(2,1)S(1)}, bf16[2,128,1024]{2,1,0:T(8,128)(2,1)S(1)}, u32[]{:S(2)}, u32[]{:S(2)}) collective-permute-start(bf16[2,128,1024]{2,1,0:T(8,128)(2,1)S(1)} %get-tuple-element.25), channel_id=1, source_target_pairs={{1,0},{2,1},{3,2},{4,3},{5,4},{6,5},{7,6},{8,7},{9,8},{10,9},{11,1... | collective-permute-start | bytes 1572872 | tf_op jit(solution)/shard_map/ppermute | solution.py:20
  14.2 4.7 %collective-permute-start = (bf16[2,128,1024]{2,1,0:T(8,128)(2,1)S(1)}, bf16[2,128,1024]{2,1,0:T(8,128)(2,1)}, u32[]{:S(2)}, u32[]{:S(2)}) collective-permute-start(bf16[2,128,1024]{2,1,0:T(8,128)(2,1)S(1)} %get-tuple-element.25), channel_id=1, source_target_pairs={{0,1},{1,2},{2,3},{3,4},{4,5},{5,6},{6,7},{7,8},{8,9},{9,10},{10,1... | collective-permute-start | bytes 1572872 | tf_op jit(solution)/shard_map/ppermute | solution.py:19
  124.3 3.3 copy-start.5
  167.9 5.0 %copy-start.3 = (f32[8,128,1024]{1,2,0:T(8,128)S(1)}, f32[8,128,1024]{1,2,0:T(8,128)}, u32[]{:S(2)}) copy-start(f32[8,128,1024]{1,2,0:T(8,128)} %get-tuple-element.29) | copy-start | bytes 12582916
  167.9 5.0 %copy-start.4 = (bf16[1024,8,128]{0,2,1:T(8,128)(2,1)S(1)}, bf16[1024,8,128]{0,2,1:T(8,128)(2,1)}, u32[]{:S(2)}) copy-start(bf16[1024,8,128]{0,2,1:T(8,128)(2,1)} %copy.52) | copy-start | bytes 6291460
  190.4 1.4 copy-start.1
  210.8 211.8 %reduce-scatter.2.cloned.1.call-start = ((), (), s32[]{:S(2)}) async-start(), calls=%async_computation.3 | async-start | bytes 8912896 | tf_op jit(solution)/shard_map/reduce_scatter | solution.py:156
  219.1 0.7 copy-start.10
  237.8 7.0 %copy-start.2 = (bf16[1024,2048]{1,0:T(8,128)(2,1)S(1)}, bf16[1024,2048]{1,0:T(8,128)(2,1)}, u32[]{:S(2)}) copy-start(bf16[1024,2048]{1,0:T(8,128)(2,1)} %all-gather.2.cloned.1.call-done) | copy-start | bytes 12582916
  240.1 73.6 %copy-start.8 = (s32[2]{0:T(128)S(1)}, s32[2]{0:T(128)}, u32[]{:S(2)}) copy-start(s32[2]{0:T(128)} %param.13) | copy-start | bytes 28
  240.2 80.0 %collective-permute-start.3 = (bf16[2,128,1024]{2,1,0:T(8,128)(2,1)S(1)}, bf16[2,128,1024]{2,1,0:T(8,128)(2,1)S(1)}, u32[]{:S(2)}, u32[]{:S(2)}) collective-permute-start(bf16[2,128,1024]{2,1,0:T(8,128)(2,1)S(1)} %get-tuple-element.20), channel_id=1, source_target_pairs={{1,0},{2,1},{3,2},{4,3},{5,4},{6,5},{7,6},{8,7},{9,8},{10,9},{11,1... | collective-permute-start | bytes 1572872 | tf_op jit(solution)/shard_map/ppermute | solution.py:20
  241.5 78.8 %collective-permute-start.2 = (bf16[2,128,1024]{2,1,0:T(8,128)(2,1)S(1)}, bf16[2,128,1024]{2,1,0:T(8,128)(2,1)S(1)}, u32[]{:S(2)}, u32[]{:S(2)}) collective-permute-start(bf16[2,128,1024]{2,1,0:T(8,128)(2,1)S(1)} %get-tuple-element.19), channel_id=1, source_target_pairs={{0,1},{1,2},{2,3},{3,4},{4,5},{5,6},{6,7},{7,8},{8,9},{9,10},{10,1... | collective-permute-start | bytes 1572872 | tf_op jit(solution)/shard_map/ppermute | solution.py:19
Sparse Core Ops, SparseCore 0:
  12.2 99.7 all-reduce.5
  114.1 49.8 all-gather.1
  210.9 102.7 all-reduce.3
  318.7 103.8 reduce-scatter.1
where the time goes:
time: 430 us; the launch traced here: 429 us
  waiting for transfers between devices  290 us (67%)
  local copies, waits for them, and re-layouts  46.4 us (11%)
  matrix products  41.4 us (10%)
  other arithmetic  26 us (6%)
  between operations  15.3 us (4%)
  starting transfers between devices  10.1 us (2%)
    reduce_scatter x1, waiting for transfers between devices, local(): lax.psum_scatter(lax.dot_general(columns, grad_out, (((0,), (0,)), ((), (...  99.8 us
    psum x1, waiting for transfers between devices, spread(): return lax.psum(jnp.where(mine, shard, jnp.zeros_like(shard)), axis)  89.4 us
    psum x1, waiting for transfers between devices, local(): global_total = lax.psum(grad_global, 'seq')  67.3 us
    all_gather x1, waiting for transfers between devices, local(): lax.all_gather(out_weight, 'seq', axis=0, tiled=True)  32.2 us
    another operation x2, local copies, waits for them, and re-layouts, fold_gradients(): stacked = jnp.stack([grad_chosen_keys, grad_chosen_values])  9.74 us
    dot_general x1, matrix products, fold_gradients(): jnp.einsum('sj,ksx->kjx', one_hot, local_part, precision=lax.Precision.HI...  9.71 us
  transfers between devices with their start and end apart: 8, of which 5 were waited for; matrix products, arithmetic and copies ran while one was open for 15% of the time, Pallas kernels for 0%

commit v1 on v0

--- a/solution.py
+++ b/solution.py
@@ -171,7 +171,7 @@
         [grad_ext[:, :tok_rows], grad_ext[:, 2 * tok_rows :]], axis=1
     ).astype(jnp.bfloat16)
     arrived = extended_2(rim_grads, (("seq", 1),), tok_rows)
-    global_total = lax.psum(grad_global, "seq")
+    global_total = jnp.sum(lax.all_gather(grad_global, "seq"), axis=0)
     owned_mask = (
         global_blocks[:, None]
         == device * blocks_dev + jnp.arange(blocks_dev, dtype=jnp.int32)[None, :]

time: 430 us -> 506 us (1.18)
  waiting for transfers between devices: 290 us -> 346 us
  other arithmetic: 26 us -> 41.1 us
  local copies, waits for them, and re-layouts: 46.4 us -> 53.5 us
    all_gather x0 -> x1, waiting for transfers between devices: none -> 138 us  [local(): global_total = jnp.sum(lax.all_gather(grad_global, 'seq'), axis=0)]
    psum x1 -> x0, waiting for transfers between devices: 67.3 us -> none  [local(): global_total = lax.psum(grad_global, 'seq')]
    reduce_sum x0 -> x1, other arithmetic: none -> 12.1 us  [local(): global_total = jnp.sum(lax.all_gather(grad_global, 'seq'), axis=0)]
    reduce_scatter x1, waiting for transfers between devices: 99.8 us -> 89.4 us  [local(): lax.psum_scatter(lax.dot_general(columns, grad_out, (((0,), (0,)), ((), (...]
    dot_general x1 -> x0, other arithmetic: 5.72 us -> none  [local(): jnp.einsum('gj,kgx->kjx', owned_mask, global_total.reshape(2, owned_mask....]
    another operation x1 -> x2, other arithmetic: 2.31 us -> 7.96 us  [the longest x1 5.68 us: fold_gradients(): stacked = jnp.stack([grad_chosen_keys, grad_chosen_values])]
    another operation x5 -> x6, local copies, waits for them, and re-layouts: 6.49 us -> 11.6 us
  transfers between devices with their start and end apart: 8 -> 8, of which waited for: 5 -> 4; matrix products, arithmetic and copies ran while one was open for 15% -> 17% of each run, Pallas kernels for 0% -> 0%
where the time goes in v1:
time: 506 us
  waiting for transfers between devices  346 us (68%)
  local copies, waits for them, and re-layouts  53.5 us (11%)
  matrix products  41.3 us (8%)
  other arithmetic  41.1 us (8%)
  between operations  15.3 us (3%)
  starting transfers between devices  8.58 us (2%)
    all_gather x1, waiting for transfers between devices, local(): global_total = jnp.sum(lax.all_gather(grad_global, 'seq'), axis=0)  138 us
    reduce_scatter x1, waiting for transfers between devices, local(): lax.psum_scatter(lax.dot_general(columns, grad_out, (((0,), (0,)), ((), (...  89.4 us
    psum x1, waiting for transfers between devices, spread(): return lax.psum(jnp.where(mine, shard, jnp.zeros_like(shard)), axis)  88.4 us
    all_gather x1, waiting for transfers between devices, local(): lax.all_gather(out_weight, 'seq', axis=0, tiled=True)  29.6 us
    reduce_sum x1, other arithmetic, local(): global_total = jnp.sum(lax.all_gather(grad_global, 'seq'), axis=0)  12.1 us
  transfers between devices with their start and end apart: 8, of which 4 were waited for; matrix products, arithmetic and copies ran while one was open for 17% of the time, Pallas kernels for 0%

profile of v1, /device:TPU:0, one launch (start us, length us, event | category | flops | bytes accessed | tf_op | source)
XLA Modules:
  0.0 505.5 jit_solution(15254236575942950469)
XLA Ops:
  7.2 0.0 all-reduce.3.cloned.1.call-start
  7.2 1.3 fusion.34
  9.8 2.1 select_bitcast_fusion.1
  11.9 0.0 all-reduce.3.cloned.1.call-update
  12.0 0.0 all-gather.3.cloned.1.call-start
  12.0 0.7 all-gather.3.cloned.1.call-update
  12.7 0.0 all-gather.5.cloned.1.call-start
  12.8 1.3 collective-permute-start.1
  14.1 3.1 collective-permute-start
  17.1 0.7 fusion.53
  17.8 0.7 fusion.28
  18.5 0.7 fusion.52
  19.2 0.7 and_bitcast_fusion
  19.9 0.1 compare_and_fusion
  20.0 0.1 fusion.25
  20.0 0.1 broadcast_bitcast_fusion
  20.1 1.2 pad_maximum_fusion.2
  21.3 2.5 gather_fusion
  23.8 88.4 %all-reduce.3.cloned.1.call-done = (bf16[1,2,128,1024]{3,2,1,0:T(8,128)(2,1)}, bf16[1,2,128,1024]{3,2,1,0:T(8,128)(2,1)}) async-done(((bf16[1,2,128,1024]{3,2,1,0:T(8,128)(2,1)}, bf16[1,2,128,1024]{3,2,1,0:T(8,128)(2,1)}), (bf16[1,2,128,1024]{3,2,1,0:T(8,128)(2,1)}, bf16[1,2,128,1024]{3,2,1,0:T(8,128)(2,1)})) %all-reduce.3.cloned.1.call-update) | async-done | bytes 1048592 | tf_op jit(solution)/shard_map/psum | solution.py:27
  112.2 1.3 maximum_bitcast_fusion.2
  113.5 2.3 bitcast_select_fusion
  115.8 1.6 pad_maximum_fusion.1
  117.3 2.0 copy.76
  119.3 3.3 copy.52
  122.6 3.6 copy.75
  126.2 4.1 copy.70
  130.3 0.8 fusion.19
  131.1 3.5 fusion.35
  134.6 29.6 %all-gather.3.cloned.1.call-done = bf16[1024,2048]{1,0:T(8,128)(2,1)} async-done(((bf16[64,2048]{1,0:T(8,128)(2,1)}), bf16[1024,2048]{1,0:T(8,128)(2,1)}) %all-gather.3.cloned.1.call-update) | async-done | bytes 4194320 | tf_op jit(solution)/shard_map/all_gather | solution.py:142
  164.3 3.7 convolution_convert_fusion.3
  168.0 0.2 copy.73
  168.2 5.0 convolution_bitcast_fusion.1
  173.2 3.1 multiply_reduce_fusion
  176.3 5.4 %copy.58 = f32[1,1024,8,128]{3,2,1,0:T(8,128)} copy(f32[1,1024,8,128]{1,3,2,0:T(8,128)} %convolution_bitcast_fusion.1) | data formatting | bytes 8388608 | tf_op jit(solution)/shard_map/qhij,qihd->qjhd/transpose | solution.py:82
  181.7 4.9 stack.34
  186.6 4.2 multiply_convert_fusion
  190.8 1.3 copy-done.1
  192.1 0.7 convolution_bitcast_fusion.2
  192.8 4.4 copy.55
  197.2 5.0 stack.33
  202.2 5.7 %pad_maximum_fusion = f32[2,1,2,131072]{3,2,0,1:T(2,128)} fusion(f32[1,1,8,131072]{3,2,0,1:T(8,128)} %bitcast.140, f32[1,1,8,131072]{3,2,0,1:T(8,128)} %bitcast.142), kind=kLoop, calls=%fused_computation.22 | loop fusion | flops 524288 | bytes 10485760 | tf_op jit(solution)/shard_map/stack | solution.py:100
  207.9 4.1 all_gather_reshape.3
  211.9 0.0 all-gather.5.cloned.1.call-update
  212.0 0.3 reduce-scatter.2.cloned.1.call-start
  212.2 3.5 convolution_convert_fusion.2
  215.8 4.6 fusion.36
  220.4 0.6 copy-done.7
  221.1 0.1 add_bitcast_fusion
  221.2 2.3 convolution_convert_fusion.1
  223.4 0.9 copy.61
  224.3 9.9 %convolution_bitcast_fusion = f32[2,3,131072]{2,1,0:T(4,128)} fusion(f32[1,1,8,131072]{3,2,0,1:T(8,128)} %bitcast.141, f32[1,1,8,131072]{3,2,0,1:T(8,128)} %bitcast.143, s32[6]{0:T(128)S(1)} %add_bitcast_fusion), kind=kOutput, calls=%fused_computation.2 | convolution fusion | flops 58195984 | bytes 11534360 | tf_op jit(solution)/shard_map/sj,ksx->kjx/dot_general | solution.py:110
  234.2 5.1 %reshape.359 = f32[2,384,1024]{2,1,0:T(8,128)} reshape(f32[2,3,131072]{2,1,0:T(4,128)} %convolution_bitcast_fusion) | data formatting | bytes 6291456 | tf_op jit(solution)/shard_map/reshape | solution.py:111
  239.3 2.3 convert.6
  241.6 1.1 fusion.33
  242.7 2.3 collective-permute-start.2
  245.0 1.6 collective-permute-start.3
  246.5 1.5 convolution_convert_fusion
  248.1 137.6 %all-gather.5.cloned.1.call-done = f32[16,2,2,128,1024]{4,3,2,1,0:T(8,128)} async-done(((f32[1,2,2,128,1024]{4,3,2,1,0:T(8,128)}), f32[16,2,2,128,1024]{4,3,2,1,0:T(8,128)}) %all-gather.5.cloned.1.call-update) | async-done | bytes 33554448 | tf_op jit(solution)/shard_map/all_gather | solution.py:174
  385.7 12.1 %reduce_sum.33 = f32[2,2,128,1024]{3,2,1,0:T(8,128)S(1)} reduce(f32[16,2,2,128,1024]{4,3,2,1,0:T(8,128)} %all-gather.5.cloned.1.call-done, f32[]{:T(128)} %constant.59.clone.1), dimensions={0}, to_apply=%region_5.6 | reduce | flops 7864320 | bytes 35651588 | tf_op jit(solution)/shard_map/reduce_sum | solution.py:174
  397.8 2.8 reshape.360
  400.7 6.1 %fusion.26 = f32[1,2,128,1024]{3,0,2,1:T(1,128)S(1)} fusion(f32[2,128,1024,2]{2,3,1,0:T(2,128)} %bitcast.149, s32[2]{0:T(128)S(1)} %copy-done.6, s32[]{:T(128)S(6)} %axis_index.8), kind=kOutput, calls=%fused_computation.61 | convolution fusion | flops 6291458 | bytes 3145740 | tf_op jit(solution)/shard_map/gj,kgx->kjx/dot_general | solution.py:179
  406.7 2.0 fusion.15
  408.8 0.8 slice_bitcast_fusion
  409.6 89.4 %reduce-scatter.2.cloned.1.call-done = f32[64,2048]{1,0:T(8,128)} async-done(((f32[1024,2048]{1,0:T(8,128)}), f32[64,2048]{1,0:T(8,128)}) %reduce-scatter.2.cloned.1.call-update) | async-done | bytes 524304 | tf_op jit(solution)/shard_map/reduce_scatter | solution.py:156
  (26 shorter events, 0.1 us)
Async XLA Ops:
  7.2 157.1 %copy-start = (bf16[128,2048]{1,0:T(8,128)(2,1)S(1)}, bf16[128,2048]{1,0:T(8,128)(2,1)}, u32[]{:S(2)}) copy-start(bf16[128,2048]{1,0:T(8,128)(2,1)} %param.12) | copy-start | bytes 1572868
  7.2 105.0 %all-reduce.3.cloned.1.call-start = ((), (), s32[]{:S(2)}) async-start(), calls=%async_computation.4 | async-start | bytes 2097152 | tf_op jit(solution)/shard_map/psum | solution.py:27
  12.0 152.3 %all-gather.3.cloned.1.call-start = ((), (), s32[]{:S(2)}) async-start(), calls=%async_computation.1 | async-start | bytes 4456448 | tf_op jit(solution)/shard_map/all_gather | solution.py:142
  12.7 372.9 %all-gather.5.cloned.1.call-start = ((), (), s32[]{:S(2)}) async-start(), calls=%async_computation.2 | async-start | bytes 35651584 | tf_op jit(solution)/shard_map/all_gather | solution.py:174
  12.8 7.3 %collective-permute-start.1 = (bf16[2,128,1024]{2,1,0:T(8,128)(2,1)S(1)}, bf16[2,128,1024]{2,1,0:T(8,128)(2,1)S(1)}, u32[]{:S(2)}, u32[]{:S(2)}) collective-permute-start(bf16[2,128,1024]{2,1,0:T(8,128)(2,1)S(1)} %get-tuple-element.30), channel_id=1, source_target_pairs={{1,0},{2,1},{3,2},{4,3},{5,4},{6,5},{7,6},{8,7},{9,8},{10,9},{11,1... | collective-permute-start | bytes 1572872 | tf_op jit(solution)/shard_map/ppermute | solution.py:20
  14.1 6.0 %collective-permute-start = (bf16[2,128,1024]{2,1,0:T(8,128)(2,1)S(1)}, bf16[2,128,1024]{2,1,0:T(8,128)(2,1)S(1)}, u32[]{:S(2)}, u32[]{:S(2)}) collective-permute-start(bf16[2,128,1024]{2,1,0:T(8,128)(2,1)S(1)} %get-tuple-element.30), channel_id=1, source_target_pairs={{0,1},{1,2},{2,3},{3,4},{4,5},{5,6},{6,7},{7,8},{8,9},{9,10},{10,1... | collective-permute-start | bytes 1572872 | tf_op jit(solution)/shard_map/ppermute | solution.py:19
  122.6 7.8 %copy-start.5 = (bf16[128,1024]{1,0:T(8,128)(2,1)S(1)}, bf16[128,1024]{1,0:T(8,128)(2,1)}, u32[]{:S(2)}) copy-start(bf16[128,1024]{1,0:T(8,128)(2,1)} %param.8) | copy-start | bytes 786436
  168.2 5.1 %copy-start.3 = (f32[8,128,1024]{1,2,0:T(8,128)S(1)}, f32[8,128,1024]{1,2,0:T(8,128)}, u32[]{:S(2)}) copy-start(f32[8,128,1024]{1,2,0:T(8,128)} %get-tuple-element.34) | copy-start | bytes 12582916
  168.2 5.1 copy-start.4
  190.7 1.4 copy-start.1
  212.0 287.0 %reduce-scatter.2.cloned.1.call-start = ((), (), s32[]{:S(2)}) async-start(), calls=%async_computation.3 | async-start | bytes 8912896 | tf_op jit(solution)/shard_map/reduce_scatter | solution.py:156
  220.4 0.7 copy-start.7
  220.4 0.7 copy-start.8
  239.3 7.2 %copy-start.2 = (bf16[1024,2048]{1,0:T(8,128)(2,1)S(1)}, bf16[1024,2048]{1,0:T(8,128)(2,1)}, u32[]{:S(2)}) copy-start(bf16[1024,2048]{1,0:T(8,128)(2,1)} %all-gather.3.cloned.1.call-done) | copy-start | bytes 12582916
  242.7 164.1 %collective-permute-start.2 = (bf16[2,128,1024]{2,1,0:T(8,128)(2,1)}, bf16[2,128,1024]{2,1,0:T(8,128)(2,1)S(1)}, u32[]{:S(2)}, u32[]{:S(2)}) collective-permute-start(bf16[2,128,1024]{2,1,0:T(8,128)(2,1)} %get-tuple-element.24), channel_id=1, source_target_pairs={{0,1},{1,2},{2,3},{3,4},{4,5},{5,6},{6,7},{7,8},{8,9},{9,10},{10,1... | collective-permute-start | bytes 1572872 | tf_op jit(solution)/shard_map/ppermute | solution.py:19
  245.0 161.8 %collective-permute-start.3 = (bf16[2,128,1024]{2,1,0:T(8,128)(2,1)}, bf16[2,128,1024]{2,1,0:T(8,128)(2,1)}, u32[]{:S(2)}, u32[]{:S(2)}) collective-permute-start(bf16[2,128,1024]{2,1,0:T(8,128)(2,1)} %get-tuple-element.25), channel_id=1, source_target_pairs={{1,0},{2,1},{3,2},{4,3},{5,4},{6,5},{7,6},{8,7},{9,8},{10,9},{11,1... | collective-permute-start | bytes 1572872 | tf_op jit(solution)/shard_map/ppermute | solution.py:20
  397.8 2.9 copy-start.6
Sparse Core Ops, SparseCore 0:
  12.1 100.0 all-reduce.2
  114.4 49.8 all-gather.2
  212.1 173.5 all-gather.4
  390.1 108.8 reduce-scatter.1
